TPU v7x, 32 devices: a whole 2x2x4 slice. The times are simulated.
32 devices in a mesh: row: 8 (over z, x), col: 4 (over y, core).
Axes of the slice: x: 2, y: 2, z: 4, core: 2. Of those that a mesh axis runs over, the one named last changes fastest.
Arguments:
- low_rhs: bfloat16 [32, 512, 128], P(('row', 'col')), may hold values from -6 to 6
- low_inv: bfloat16 [32, 512, 512], P(('row', 'col'))
- low_tiles: bfloat16 [32, 4, 512, 512], P(('row', 'col')), may hold values from -0.03125 to 0.03125
- tile_rows: int32 [32, 4], P(('row', 'col')), may hold values from -1 to 3, as said below
- tile_cols: int32 [32, 4], P(('row', 'col')), may hold values from 0 to 31, as said below
- top_rhs: bfloat16 [4, 512, 128], P(None, 'row'), may hold values from -6 to 6
- top_inv: bfloat16 [4, 512, 512], P(None, 'row')
- top_tiles: bfloat16 [6, 512, 512], P(None, 'row'), may hold values from -0.125 to 0.125
Outputs:
- low_solution: float32 [32, 512, 128], P(('row', 'col'))
- top_solution: float32 [4, 512, 128], P(None, 'row')
Inputs may be any that keep to these rules, and one draw needn't show every extreme that they name: `tile_rows`: in each block's list of 4 slots the used slots come first and name top-level blocks; the remaining slots hold -1. Some list has only its first slot used and some list is full. Slot s of block j names a block of j's aligned group of 4 blocks (j // 4 == tile_cols[j, s] // 4); an empty slot names j itself.
All inputs are finite; a program needn't handle non-finite values.
Results may differ from a plain program's by a relative error of at most 0.022.
Values may be sent and summed in bfloat16 or wider, within the bound.
No kernel may reach another device: no remote copies, remote signals or barrier semaphores. Data moves between devices by JAX's collectives and lax.ppermute only.
A program may use at most 64 MiB of HBM per device.

v0:
```python
import jax
import jax.numpy as jnp
from jax import lax
from jax.sharding import PartitionSpec as P


def local(low_rhs, low_inv, low_tiles, tile_rows, tile_cols, top_rhs, top_inv, top_tiles):
    peers = lax.axis_size("col")
    levels = top_rhs.shape[0]
    share = top_rhs.shape[1]
    position = lax.axis_index("row")
    slot_rows = tile_rows[0]
    slot_cols = tile_cols[0] % peers
    alive = slot_rows >= 0
    safe_rows = jnp.maximum(slot_rows, 0)
    own_tiles = low_tiles[0]
    low_forward = jnp.dot(low_inv[0], low_rhs[0], preferred_element_type=jnp.float32).astype(
        jnp.bfloat16
    )
    panels = lax.all_gather(low_forward[None], "col", axis=0, tiled=True)
    products = jnp.einsum(
        "sab,sbk->sak", own_tiles, panels[slot_cols], preferred_element_type=jnp.float32
    )
    pick_level = (slot_rows[:, None] == jnp.arange(levels, dtype=jnp.int32)[None, :]).astype(
        jnp.float32
    )
    coupling = jnp.einsum("st,sak->tak", pick_level, products, precision=lax.Precision.HIGHEST)
    whole_sum = lax.psum(coupling.astype(jnp.bfloat16), "col")
    coupled = lax.psum_scatter(whole_sum, "row", scatter_dimension=1, tiled=True).astype(
        jnp.float32
    )
    top_back = [None] * levels
    top_slices = [None] * levels
    top_forward = []
    for level in range(levels):
        residue = top_rhs[level].astype(jnp.float32) - coupled[level]
        if level > 0:
            first = level * (level - 1) // 2
            earlier = jnp.stack(top_forward)
            residue = residue - jnp.einsum(
                "uab,ubk->ak",
                top_tiles[first : first + level],
                earlier,
                preferred_element_type=jnp.float32,
            )
        whole_residue = lax.all_gather(residue.astype(jnp.bfloat16), "row", axis=0, tiled=True)
        solved_part = jnp.dot(
            top_inv[level], whole_residue, preferred_element_type=jnp.float32
        ).astype(jnp.bfloat16)
        top_forward.append(lax.all_gather(solved_part, "row", axis=0, tiled=True))
    for level in reversed(range(levels)):
        update = lax.dynamic_slice_in_dim(top_forward[level], position * share, share, 0).astype(
            jnp.float32
        )
        if level < levels - 1:
            later = list(range(level + 1, levels))
            tiles_below = jnp.stack([top_tiles[k * (k - 1) // 2 + level] for k in later])
            slices_below = jnp.stack(
                [lax.dynamic_slice_in_dim(top_back[k], position * share, share, 0) for k in later]
            )
            partial_term = jnp.einsum(
                "kab,kac->bc", tiles_below, slices_below, preferred_element_type=jnp.float32
            )
            update = update - lax.psum_scatter(
                partial_term.astype(jnp.bfloat16), "row", scatter_dimension=0, tiled=True
            ).astype(jnp.float32)
        local_part = jnp.einsum(
            "ab,ac->bc",
            top_inv[level],
            update.astype(jnp.bfloat16),
            preferred_element_type=jnp.float32,
        )
        solution = lax.psum(local_part.astype(jnp.bfloat16), "row").astype(jnp.float32)
        top_slices[level] = lax.dynamic_slice_in_dim(solution, position * share, share, 0)
        top_back[level] = solution.astype(jnp.bfloat16)
    back_stack = jnp.stack(top_back)
    products_back = jnp.einsum(
        "sab,sak->sbk", own_tiles, back_stack[safe_rows], preferred_element_type=jnp.float32
    )
    pick_peer = (
        (slot_cols[:, None] == jnp.arange(peers, dtype=jnp.int32)[None, :]) & alive[:, None]
    ).astype(jnp.float32)
    terms = jnp.einsum("sp,sbk->pbk", pick_peer, products_back, precision=lax.Precision.HIGHEST)
    returned = lax.psum_scatter(
        terms.astype(jnp.bfloat16), "col", scatter_dimension=0, tiled=True
    ).astype(jnp.float32)
    low_update = (low_forward.astype(jnp.float32) - returned[0]).astype(jnp.bfloat16)
    low_solution = jnp.einsum(
        "ab,ac->bc", low_inv[0], low_update, preferred_element_type=jnp.float32
    )
    return (low_solution[None], jnp.stack(top_slices))


def solution(mesh):
    in_specs = (
        P(("row", "col"), None, None),
        P(("row", "col"), None, None),
        P(("row", "col"), None, None, None),
        P(("row", "col"), None),
        P(("row", "col"), None),
        P(None, "row", None),
        P(None, "row", None),
        P(None, "row", None),
    )
    out_specs = (P(("row", "col"), None, None), P(None, "row", None))
    return jax.shard_map(local, mesh=mesh, in_specs=in_specs, out_specs=out_specs, check_vma=False)
```

profile of v0, /device:TPU:0, one launch (start us, length us, event | category | flops | bytes accessed | tf_op | source)
XLA Modules:
  0.0 905.1 jit_solution(3152110872918101658)
XLA Ops:
  7.2 1.5 convolution_convert_fusion.1
  8.7 8.7 all-gather
  17.4 0.7 fusion.99
  18.1 1.4 gather_fusion
  19.5 1.9 fusion.4
  21.4 1.3 copy.37
  22.7 3.2 convolution_convert_fusion
  26.0 0.6 dynamic-slice
  27.2 72.4 %all-reduce.18.cloned.1.call-done = bf16[4,512,128]{2,0,1:T(4,128)(2,1)} async-done(((bf16[4,512,128]{2,0,1:T(4,128)(2,1)}), bf16[4,512,128]{2,0,1:T(4,128)(2,1)}) %all-reduce.18.cloned.1.call-update) | async-done | bytes 524304
  99.6 0.9 constant_dynamic-slice_fusion.3
  100.5 0.6 copy.38
  101.2 32.1 %all-reduce.16.cloned.1.call-done = bf16[4,64,128]{2,1,0:T(8,128)(2,1)} async-done(((bf16[4,64,128]{2,1,0:T(8,128)(2,1)}), bf16[4,64,128]{2,1,0:T(8,128)(2,1)}) %all-reduce.16.cloned.1.call-update) | async-done | bytes 65552 | tf_op jit(solution)/shard_map/psum | solution.py:28
  133.2 0.8 convert_element_type.161
  134.1 30.7 %all-gather.1 = bf16[1,512,128]{2,1,0:T(8,128)(2,1)S(1)} all-gather(bf16[1,64,128]{2,1,0:T(8,128)(2,1)S(1)} %fusion.76), channel_id=3, replica_groups=mesh['row'=8,'col'=4] {'row'}, dimensions={1}, use_global_device_ids=true | all-gather | bytes 147456 | tf_op jit(solution)/shard_map/all_gather | solution.py:46
  164.8 0.2 fusion.23
  164.9 30.6 %all_gather.29 = bf16[512,128]{1,0:T(8,128)(2,1)S(1)} all-gather(bf16[64,128]{1,0:T(8,128)(2,1)S(1)} %fusion.23), channel_id=1, replica_groups=mesh['row'=8,'col'=4] {'row'}, dimensions={0}, use_global_device_ids=true | all-gather | bytes 147456 | tf_op jit(solution)/shard_map/all_gather | solution.py:50
  195.5 0.2 fusion.20
  195.6 30.5 %all_gather.30 = bf16[512,128]{1,0:T(8,128)(2,1)S(1)} all-gather(bf16[64,128]{1,0:T(8,128)(2,1)S(1)} %fusion.20), channel_id=1, replica_groups=mesh['row'=8,'col'=4] {'row'}, dimensions={0}, use_global_device_ids=true | all-gather | bytes 147456 | tf_op jit(solution)/shard_map/all_gather | solution.py:46
  226.2 0.2 fusion.24
  226.3 30.6 %all_gather.31 = bf16[512,128]{1,0:T(8,128)(2,1)S(1)} all-gather(bf16[64,128]{1,0:T(8,128)(2,1)S(1)} %fusion.24), channel_id=1, replica_groups=mesh['row'=8,'col'=4] {'row'}, dimensions={0}, use_global_device_ids=true | all-gather | bytes 147456 | tf_op jit(solution)/shard_map/all_gather | solution.py:50
  256.9 0.2 fusion.22
  257.1 30.6 %all_gather.32 = bf16[512,128]{1,0:T(8,128)(2,1)S(1)} all-gather(bf16[64,128]{1,0:T(8,128)(2,1)S(1)} %fusion.22), channel_id=1, replica_groups=mesh['row'=8,'col'=4] {'row'}, dimensions={0}, use_global_device_ids=true | all-gather | bytes 147456 | tf_op jit(solution)/shard_map/all_gather | solution.py:46
  287.7 0.2 fusion.25
  287.8 30.6 %all_gather.33 = bf16[512,128]{1,0:T(8,128)(2,1)S(1)} all-gather(bf16[64,128]{1,0:T(8,128)(2,1)S(1)} %fusion.25), channel_id=1, replica_groups=mesh['row'=8,'col'=4] {'row'}, dimensions={0}, use_global_device_ids=true | all-gather | bytes 147456 | tf_op jit(solution)/shard_map/all_gather | solution.py:50
  318.4 1.0 fusion.21
  319.4 30.5 %all_gather.34 = bf16[512,128]{1,0:T(8,128)(2,1)S(1)} all-gather(bf16[64,128]{1,0:T(8,128)(2,1)S(1)} %fusion.21), channel_id=1, replica_groups=mesh['row'=8,'col'=4] {'row'}, dimensions={0}, use_global_device_ids=true | all-gather | bytes 147456 | tf_op jit(solution)/shard_map/all_gather | solution.py:46
  349.9 0.2 fusion.26
  350.1 30.5 %all_gather.35 = bf16[512,128]{1,0:T(8,128)(2,1)S(1)} all-gather(bf16[64,128]{1,0:T(8,128)(2,1)S(1)} %fusion.26), channel_id=1, replica_groups=mesh['row'=8,'col'=4] {'row'}, dimensions={0}, use_global_device_ids=true | all-gather | bytes 147456 | tf_op jit(solution)/shard_map/all_gather | solution.py:50
  380.6 0.9 fusion.12
  381.5 70.7 %all-reduce.8.cloned.1.call-done = bf16[512,128]{0,1:T(8,128)(2,1)} async-done(((bf16[512,128]{0,1:T(8,128)(2,1)}), bf16[512,128]{0,1:T(8,128)(2,1)}) %all-reduce.8.cloned.1.call-update) | async-done | bytes 131088 | tf_op jit(solution)/shard_map/psum | solution.py:73
  452.2 0.9 constant_dynamic-slice_fusion.2
  453.1 0.9 fusion.13
  454.1 62.9 %reduce-scatter.5.cloned.1.call-done = bf16[64,128]{1,0:T(8,128)(2,1)} async-done(((bf16[512,128]{1,0:T(8,128)(2,1)}), bf16[64,128]{1,0:T(8,128)(2,1)}) %reduce-scatter.5.cloned.1.call-update) | async-done | bytes 16400 | tf_op jit(solution)/shard_map/reduce_scatter | solution.py:64
  516.9 1.6 fusion.14
  518.6 0.7 fusion.104
  519.3 0.1 copy.41
  519.3 70.9 %all-reduce.10.cloned.1.call-done = bf16[512,128]{0,1:T(8,128)(2,1)} async-done(((bf16[512,128]{0,1:T(8,128)(2,1)}), bf16[512,128]{0,1:T(8,128)(2,1)}) %all-reduce.10.cloned.1.call-update) | async-done | bytes 131088 | tf_op jit(solution)/shard_map/psum | solution.py:73
  590.3 0.9 constant_dynamic-slice_fusion.1
  591.2 0.1 copy.40
  591.3 1.8 fusion.10
  593.1 61.9 %reduce-scatter.7.cloned.1.call-done = bf16[64,128]{1,0:T(8,128)(2,1)} async-done(((bf16[512,128]{1,0:T(8,128)(2,1)}), bf16[64,128]{1,0:T(8,128)(2,1)}) %reduce-scatter.7.cloned.1.call-update) | async-done | bytes 16400 | tf_op jit(solution)/shard_map/reduce_scatter | solution.py:64
  655.0 1.6 fusion.15
  656.7 71.8 %all-reduce.12.cloned.1.call-done = bf16[512,128]{0,1:T(8,128)(2,1)} async-done(((bf16[512,128]{0,1:T(8,128)(2,1)}), bf16[512,128]{0,1:T(8,128)(2,1)}) %all-reduce.12.cloned.1.call-update) | async-done | bytes 131088 | tf_op jit(solution)/shard_map/psum | solution.py:73
  728.5 0.8 constant_dynamic-slice_fusion
  729.3 0.1 copy.42
  729.4 1.8 fusion.11
  731.3 62.1 %reduce-scatter.9.cloned.1.call-done = bf16[64,128]{1,0:T(8,128)(2,1)} async-done(((bf16[512,128]{1,0:T(8,128)(2,1)}), bf16[64,128]{1,0:T(8,128)(2,1)}) %reduce-scatter.9.cloned.1.call-update) | async-done | bytes 16400 | tf_op jit(solution)/shard_map/reduce_scatter | solution.py:64
  793.4 1.6 fusion.16
  795.1 71.8 %all-reduce.14.cloned.1.call-done = bf16[512,128]{0,1:T(8,128)(2,1)} async-done(((bf16[512,128]{0,1:T(8,128)(2,1)}), bf16[512,128]{0,1:T(8,128)(2,1)}) %all-reduce.14.cloned.1.call-update) | async-done | bytes 131088 | tf_op jit(solution)/shard_map/psum | solution.py:73
  866.9 1.0 pad_maximum_fusion
  868.0 1.4 gather_fusion.1
  869.3 1.5 fusion.7
  870.8 1.3 copy.43
  872.1 2.4 fusion.90
  874.5 0.9 copy.53
  875.4 0.1 copy.48
  875.5 0.1 copy.47
  875.6 0.1 copy.46
  875.7 0.9 dynamic-slice_convert_fusion
  876.5 0.1 copy.45
  876.6 0.7 pad_maximum_fusion.1
  877.3 19.0 %reduce-scatter.11.cloned.1.call-done = bf16[1,512,128]{2,1,0:T(8,128)(2,1)} async-done(((bf16[4,512,128]{2,1,0:T(8,128)(2,1)}), bf16[1,512,128]{2,1,0:T(8,128)(2,1)}) %reduce-scatter.11.cloned.1.call-update) | async-done | bytes 131088 | tf_op jit(solution)/shard_map/reduce_scatter | solution.py:84
  896.3 1.2 convolution_bitcast_fusion
  897.5 0.8 copy.49
  (62 shorter events, 0.7 us)
Async XLA Ops:
  7.2 12.3 %copy-start = (bf16[1,4,512,512]{3,2,1,0:T(8,128)(2,1)S(1)}, bf16[1,4,512,512]{3,2,1,0:T(8,128)(2,1)}, u32[]{:S(2)}) copy-start(bf16[1,4,512,512]{3,2,1,0:T(8,128)(2,1)} %param.10) | copy-start | bytes 6291460
  7.2 92.4 %all-reduce.18.cloned.1.call-start = ((), (), s32[]{:S(2)}) async-start(), calls=%async_computation.13 | async-start | bytes 1048576
  19.5 3.2 copy-start.14
  21.4 4.6 copy-start.16
  21.4 143.4 %copy-start.2 = (bf16[4,64,512]{2,1,0:T(8,128)(2,1)S(1)}, bf16[4,64,512]{2,1,0:T(8,128)(2,1)}, u32[]{:S(2)}) copy-start(bf16[4,64,512]{2,1,0:T(8,128)(2,1)} %param.14) | copy-start | bytes 786436
  22.7 111.4 %copy-start.13 = (bf16[4,64,128]{2,1,0:T(8,128)(2,1)S(1)}, bf16[4,64,128]{2,1,0:T(8,128)(2,1)}, u32[]{:S(2)}) copy-start(bf16[4,64,128]{2,1,0:T(8,128)(2,1)} %param.13) | copy-start | bytes 196612
  22.7 172.7 %copy-start.3 = (bf16[6,64,512]{2,1,0:T(8,128)(2,1)S(1)}, bf16[6,64,512]{2,1,0:T(8,128)(2,1)}, u32[]{:S(2)}) copy-start(bf16[6,64,512]{2,1,0:T(8,128)(2,1)} %param.15) | copy-start | bytes 1179652
  25.9 107.3 %all-reduce.16.cloned.1.call-start = ((), (), s32[]{:S(2)}) async-start(), calls=%async_computation.12 | async-start | bytes 131072 | tf_op jit(solution)/shard_map/psum | solution.py:28
  101.1 351.1 %all-reduce.8.cloned.1.call-start = ((), (), s32[]{:S(2)}) async-start(), calls=%async_computation.4 | async-start | bytes 262144 | tf_op jit(solution)/shard_map/psum | solution.py:73
  256.9 124.6 %copy-start.12 = (bf16[512,128]{1,0:T(8,128)(2,1)}, bf16[512,128]{1,0:T(8,128)(2,1)S(1)}, u32[]{:S(2)}) copy-start(bf16[512,128]{1,0:T(8,128)(2,1)S(1)} %all_gather.31) | copy-start | bytes 393220
  318.4 411.0 %slice-start = ((bf16[6,64,512]{2,1,0:T(8,128)(2,1)}), bf16[2,64,512]{2,1,0:T(8,128)(2,1)S(1)}, s32[]{:S(2)}) async-start(bf16[6,64,512]{2,1,0:T(8,128)(2,1)} %param.15), calls=%async_computation.14 | async-start | bytes 262144 | tf_op jit(solution)/shard_map/slice | solution.py:57
  319.4 411.9 %copy-start.15 = (s32[1,4]{1,0:T(1,128)S(1)}, s32[1,4]{1,0:T(1,128)}, u32[]{:S(2)}) copy-start(s32[1,4]{1,0:T(1,128)} %param.12) | copy-start | bytes 52
  381.5 135.4 %reduce-scatter.5.cloned.1.call-start = ((), (), s32[]{:S(2)}) async-start(), calls=%async_computation.5 | async-start | bytes 147456 | tf_op jit(solution)/shard_map/reduce_scatter | solution.py:64
  452.2 414.7 %copy-start.10 = (bf16[512,128]{0,1:T(8,128)(2,1)S(1)}, bf16[512,128]{0,1:T(8,128)(2,1)}, u32[]{:S(2)}) copy-start(bf16[512,128]{0,1:T(8,128)(2,1)} %all-reduce.8.cloned.1.call-done) | copy-start | bytes 393220
  453.1 414.8 %copy-start.4 = (bf16[64,128]{0,1:T(8,128)(2,1)}, bf16[64,128]{0,1:T(8,128)(2,1)S(1)}, u32[]{:S(2)}) copy-start(bf16[64,128]{0,1:T(8,128)(2,1)S(1)} %constant_dynamic-slice_fusion.2) | copy-start | bytes 49156
  454.0 136.2 %all-reduce.10.cloned.1.call-start = ((), (), s32[]{:S(2)}) async-start(), calls=%async_computation.6 | async-start | bytes 262144 | tf_op jit(solution)/shard_map/psum | solution.py:73
  518.5 136.5 %reduce-scatter.7.cloned.1.call-start = ((), (), s32[]{:S(2)}) async-start(), calls=%async_computation.7 | async-start | bytes 147456 | tf_op jit(solution)/shard_map/reduce_scatter | solution.py:64
  590.3 276.6 %copy-start.11 = (bf16[512,128]{0,1:T(8,128)(2,1)S(1)}, bf16[512,128]{0,1:T(8,128)(2,1)}, u32[]{:S(2)}) copy-start(bf16[512,128]{0,1:T(8,128)(2,1)} %all-reduce.10.cloned.1.call-done) | copy-start | bytes 393220
  591.2 276.8 %copy-start.6 = (bf16[64,128]{0,1:T(8,128)(2,1)}, bf16[64,128]{0,1:T(8,128)(2,1)S(1)}, u32[]{:S(2)}) copy-start(bf16[64,128]{0,1:T(8,128)(2,1)S(1)} %constant_dynamic-slice_fusion.1) | copy-start | bytes 49156
  593.0 135.4 %all-reduce.12.cloned.1.call-start = ((), (), s32[]{:S(2)}) async-start(), calls=%async_computation.8 | async-start | bytes 262144 | tf_op jit(solution)/shard_map/psum | solution.py:73
  656.6 136.8 %reduce-scatter.9.cloned.1.call-start = ((), (), s32[]{:S(2)}) async-start(), calls=%async_computation.9 | async-start | bytes 147456 | tf_op jit(solution)/shard_map/reduce_scatter | solution.py:64
  729.3 138.6 %copy-start.8 = (bf16[64,128]{0,1:T(8,128)(2,1)}, bf16[64,128]{0,1:T(8,128)(2,1)S(1)}, u32[]{:S(2)}) copy-start(bf16[64,128]{0,1:T(8,128)(2,1)S(1)} %constant_dynamic-slice_fusion) | copy-start | bytes 49156
  731.2 135.7 %all-reduce.14.cloned.1.call-start = ((), (), s32[]{:S(2)}) async-start(), calls=%async_computation.10 | async-start | bytes 262144 | tf_op jit(solution)/shard_map/psum | solution.py:73
  795.0 101.3 %reduce-scatter.11.cloned.1.call-start = ((), (), s32[]{:S(2)}) async-start(), calls=%async_computation.11 | async-start | bytes 655360 | tf_op jit(solution)/shard_map/reduce_scatter | solution.py:84
  872.1 3.3 copy-start.5
  872.1 3.3 copy-start.7
  872.1 3.4 copy-start.9
  872.1 24.2 %copy-start.1 = (bf16[1,512,512]{2,1,0:T(8,128)(2,1)S(1)}, bf16[1,512,512]{2,1,0:T(8,128)(2,1)}, u32[]{:S(2)}) copy-start(bf16[1,512,512]{2,1,0:T(8,128)(2,1)} %param.9) | copy-start | bytes 1572868
Sparse Core Ops, SparseCore 0:
  26.0 73.4 all-reduce.17
  102.5 30.7 all-reduce.15
  381.6 70.5 all-reduce.7
  455.9 60.9 reduce-scatter.4
  520.7 69.5 all-reduce.9
  594.0 60.9 reduce-scatter.6
  658.9 69.5 all-reduce.11
  732.4 60.9 reduce-scatter.8
  797.3 69.5 all-reduce.13
  875.5 20.7 reduce-scatter.10
where the time goes:
time: 906 us; the launch traced here: 905 us
  waiting for transfers between devices  596 us (66%)
  blocking collectives  253 us (28%)
  matrix products  23.5 us (3%)
  between operations  15.1 us (2%)
  local copies, waits for them, and re-layouts  13.2 us (1%)
    psum x4, waiting for transfers between devices, local(): lax.psum(local_part.astype(jnp.bfloat16), 'row').astype(jnp.float32)  285 us
    reduce_scatter x3, waiting for transfers between devices, local(): lax.psum_scatter(partial_term.astype(jnp.bfloat16), 'row', scatter_dimens...  187 us
    all_gather x4, blocking collectives, local(): lax.all_gather(residue.astype(jnp.bfloat16), 'row', axis=0, tiled=True)  122 us
    all_gather x4, blocking collectives, local(): top_forward.append(lax.all_gather(solved_part, 'row', axis=0, tiled=True))  122 us
    unnamed x11, waiting for transfers between devices  72.5 us
    psum x1, waiting for transfers between devices, local(): whole_sum = lax.psum(coupling.astype(jnp.bfloat16), 'col')  32.1 us
    reduce_scatter x1, waiting for transfers between devices, local(): lax.psum_scatter(terms.astype(jnp.bfloat16), 'col', scatter_dimension=0,...  19 us
  transfers between devices with their start and end apart: 10, of which 10 were waited for; matrix products, arithmetic and copies ran while one was open for 0% of the time, Pallas kernels for 0%

commit v1 on v0

--- a/solution.py
+++ b/solution.py
@@ -2,6 +2,21 @@
 import jax.numpy as jnp
 from jax import lax
 from jax.sharding import PartitionSpec as P
+
+
+def manage_the_panels(inputs):
+    lane_axis = "row"
+    n_shards = lax.axis_size(lane_axis)
+    sides = tuple(((dd, (dd + 1) % n_shards) for dd in range(n_shards)))
+    parts_seen = tuple(((dd, (dd - 1) % n_shards) for dd in range(n_shards)))
+    s_next, opened = ([inputs], [inputs])
+    for _ in range(n_shards // 2):
+        s_next.append(lax.ppermute(s_next[-1], lane_axis, sides))
+    for _ in range((n_shards - 1) // 2):
+        w_next = lax.ppermute(opened[-1], lane_axis, parts_seen)
+        opened.append(w_next)
+    after = jnp.concatenate([*s_next[::-1], *opened[1:]], axis=0)
+    return jnp.roll(after, (lax.axis_index(lane_axis) - n_shards // 2) * inputs.shape[0], axis=0)
 
 
 def local(low_rhs, low_inv, low_tiles, tile_rows, tile_cols, top_rhs, top_inv, top_tiles):
@@ -47,7 +62,7 @@
         solved_part = jnp.dot(
             top_inv[level], whole_residue, preferred_element_type=jnp.float32
         ).astype(jnp.bfloat16)
-        top_forward.append(lax.all_gather(solved_part, "row", axis=0, tiled=True))
+        top_forward.append(manage_the_panels(solved_part))
     for level in reversed(range(levels)):
         update = lax.dynamic_slice_in_dim(top_forward[level], position * share, share, 0).astype(
             jnp.float32

time: 906 us -> 892 us (0.985)
  blocking collectives: 253 us -> 131 us
  starting transfers between devices: 0.41 us -> 64.7 us
  waiting for transfers between devices: 596 us -> 630 us
    all_gather x4 -> x0, blocking collectives: 122 us -> none  [local(): top_forward.append(lax.all_gather(solved_part, 'row', axis=0, tiled=True))]
    ppermute x0 -> x28, starting transfers between devices: none -> 64.3 us  [the longest x12 56.8 us: manage_the_panels(): w_next = lax.ppermute(opened[-1], lane_axis, parts_seen)]
    ppermute x0 -> x28, waiting for transfers between devices: none -> 38.6 us  [the longest x16 38.4 us: manage_the_panels(): s_next.append(lax.ppermute(s_next[-1], lane_axis, sides))]
  transfers between devices with their start and end apart: 10 -> 38, of which waited for: 10 -> 27; matrix products, arithmetic and copies ran while one was open for 0% -> 1% of each run, Pallas kernels for 0% -> 0%
where the time goes in v1:
time: 892 us; the launch traced here: 890 us
  waiting for transfers between devices  630 us (71%)
  blocking collectives  131 us (15%)
  starting transfers between devices  64.7 us (7%)
  matrix products  24.6 us (3%)
  local copies, waits for them, and re-layouts  17.6 us (2%)
  between operations  15.2 us (2%)
    psum x4, waiting for transfers between devices, local(): lax.psum(local_part.astype(jnp.bfloat16), 'row').astype(jnp.float32)  282 us
    reduce_scatter x3, waiting for transfers between devices, local(): lax.psum_scatter(partial_term.astype(jnp.bfloat16), 'row', scatter_dimens...  185 us
    all_gather x4, blocking collectives, local(): lax.all_gather(residue.astype(jnp.bfloat16), 'row', axis=0, tiled=True)  123 us
    unnamed x11, waiting for transfers between devices  72.5 us
    ppermute x12, starting transfers between devices, manage_the_panels(): w_next = lax.ppermute(opened[-1], lane_axis, parts_seen)  56.8 us
    ppermute x16, waiting for transfers between devices, manage_the_panels(): s_next.append(lax.ppermute(s_next[-1], lane_axis, sides))  38.4 us
    psum x1, waiting for transfers between devices, local(): whole_sum = lax.psum(coupling.astype(jnp.bfloat16), 'col')  32.1 us
    reduce_scatter x1, waiting for transfers between devices, local(): lax.psum_scatter(terms.astype(jnp.bfloat16), 'col', scatter_dimension=0,...  19 us
  transfers between devices with their start and end apart: 38, of which 27 were waited for; matrix products, arithmetic and copies ran while one was open for 1% of the time, Pallas kernels for 0%

profile of v1, /device:TPU:0, one launch (start us, length us, event | category | flops | bytes accessed | tf_op | source)
XLA Modules:
  0.0 890.1 jit_solution(7792175258752948883)
XLA Ops:
  7.2 1.5 convolution_convert_fusion.1
  8.7 8.7 all-gather
  18.1 1.4 gather_fusion
  19.5 1.9 fusion.4
  21.4 1.3 copy.37
  22.8 3.2 convolution_convert_fusion
  27.3 72.4 %all-reduce.18.cloned.1.call-done = bf16[4,512,128]{2,0,1:T(4,128)(2,1)} async-done(((bf16[4,512,128]{2,0,1:T(4,128)(2,1)}), bf16[4,512,128]{2,0,1:T(4,128)(2,1)}) %all-reduce.18.cloned.1.call-update) | async-done | bytes 524304
  101.2 32.1 %all-reduce.16.cloned.1.call-done = bf16[4,64,128]{2,1,0:T(8,128)(2,1)} async-done(((bf16[4,64,128]{2,1,0:T(8,128)(2,1)}), bf16[4,64,128]{2,1,0:T(8,128)(2,1)}) %all-reduce.16.cloned.1.call-update) | async-done | bytes 65552 | tf_op jit(solution)/shard_map/psum | solution.py:43
  134.1 30.7 %all-gather.1 = bf16[1,512,128]{2,1,0:T(8,128)(2,1)S(1)} all-gather(bf16[1,64,128]{2,1,0:T(8,128)(2,1)S(1)} %fusion.81), channel_id=3, replica_groups=mesh['row'=8,'col'=4] {'row'}, dimensions={1}, use_global_device_ids=true | all-gather | bytes 147456 | tf_op jit(solution)/shard_map/all_gather | solution.py:61
  164.9 1.5 collective-permute-start
  166.4 5.0 collective-permute-done
  171.4 4.7 collective-permute-start.4
  176.2 1.7 collective-permute-done.1
  177.9 4.7 collective-permute-start.5
  182.6 1.7 collective-permute-done.2
  184.3 4.7 collective-permute-start.6
  189.0 1.7 collective-permute-done.3
  191.4 30.5 %all_gather.17 = bf16[512,128]{1,0:T(8,128)(2,1)S(1)} all-gather(bf16[64,128]{1,0:T(8,128)(2,1)S(1)} %fusion.20), channel_id=1, replica_groups=mesh['row'=8,'col'=4] {'row'}, dimensions={0}, use_global_device_ids=true | all-gather | bytes 147456 | tf_op jit(solution)/shard_map/all_gather | solution.py:61
  222.1 2.0 collective-permute-start.7
  224.1 4.5 collective-permute-done.7
  228.6 4.7 collective-permute-start.11
  233.3 1.7 collective-permute-done.8
  235.0 4.7 collective-permute-start.12
  239.8 1.7 collective-permute-done.9
  241.9 4.8 collective-permute-start.13
  246.7 1.2 collective-permute-done.10
  249.5 30.8 %all_gather.18 = bf16[512,128]{1,0:T(8,128)(2,1)S(1)} all-gather(bf16[64,128]{1,0:T(8,128)(2,1)S(1)} %fusion.22), channel_id=1, replica_groups=mesh['row'=8,'col'=4] {'row'}, dimensions={0}, use_global_device_ids=true | all-gather | bytes 147456 | tf_op jit(solution)/shard_map/all_gather | solution.py:61
  280.5 2.0 collective-permute-start.14
  282.6 4.5 collective-permute-done.14
  287.0 4.7 collective-permute-start.18
  291.7 1.7 collective-permute-done.15
  293.5 4.7 collective-permute-start.19
  298.2 1.7 collective-permute-done.16
  299.9 4.7 collective-permute-start.20
  304.6 1.7 collective-permute-done.17
  307.8 30.7 %all_gather.19 = bf16[512,128]{1,0:T(8,128)(2,1)S(1)} all-gather(bf16[64,128]{1,0:T(8,128)(2,1)S(1)} %fusion.21), channel_id=1, replica_groups=mesh['row'=8,'col'=4] {'row'}, dimensions={0}, use_global_device_ids=true | all-gather | bytes 147456 | tf_op jit(solution)/shard_map/all_gather | solution.py:61
  338.6 2.0 collective-permute-start.21
  340.6 4.5 collective-permute-done.21
  345.1 4.7 collective-permute-start.25
  349.9 1.7 collective-permute-done.22
  351.6 4.7 collective-permute-start.26
  356.3 1.7 collective-permute-done.23
  358.0 4.8 collective-permute-start.27
  362.9 1.7 collective-permute-done.24
  368.9 0.9 fusion.12
  369.9 67.1 %all-reduce.8.cloned.1.call-done = bf16[512,128]{0,1:T(8,128)(2,1)} async-done(((bf16[512,128]{0,1:T(8,128)(2,1)}), bf16[512,128]{0,1:T(8,128)(2,1)}) %all-reduce.8.cloned.1.call-update) | async-done | bytes 131088 | tf_op jit(solution)/shard_map/psum | solution.py:88
  438.8 62.9 %reduce-scatter.5.cloned.1.call-done = bf16[64,128]{1,0:T(8,128)(2,1)} async-done(((bf16[512,128]{1,0:T(8,128)(2,1)}), bf16[64,128]{1,0:T(8,128)(2,1)}) %reduce-scatter.5.cloned.1.call-update) | async-done | bytes 16400 | tf_op jit(solution)/shard_map/reduce_scatter | solution.py:79
  501.8 1.6 fusion.14
  503.6 71.5 %all-reduce.10.cloned.1.call-done = bf16[512,128]{0,1:T(8,128)(2,1)} async-done(((bf16[512,128]{0,1:T(8,128)(2,1)}), bf16[512,128]{0,1:T(8,128)(2,1)}) %all-reduce.10.cloned.1.call-update) | async-done | bytes 131088 | tf_op jit(solution)/shard_map/psum | solution.py:88
  576.6 1.6 fusion.10
  578.3 61.5 %reduce-scatter.7.cloned.1.call-done = bf16[64,128]{1,0:T(8,128)(2,1)} async-done(((bf16[512,128]{1,0:T(8,128)(2,1)}), bf16[64,128]{1,0:T(8,128)(2,1)}) %reduce-scatter.7.cloned.1.call-update) | async-done | bytes 16400 | tf_op jit(solution)/shard_map/reduce_scatter | solution.py:79
  639.8 1.6 fusion.15
  641.6 71.8 %all-reduce.12.cloned.1.call-done = bf16[512,128]{0,1:T(8,128)(2,1)} async-done(((bf16[512,128]{0,1:T(8,128)(2,1)}), bf16[512,128]{0,1:T(8,128)(2,1)}) %all-reduce.12.cloned.1.call-update) | async-done | bytes 131088 | tf_op jit(solution)/shard_map/psum | solution.py:88
  714.3 1.7 fusion.11
  717.3 60.9 %reduce-scatter.9.cloned.1.call-done = bf16[64,128]{1,0:T(8,128)(2,1)} async-done(((bf16[512,128]{1,0:T(8,128)(2,1)}), bf16[64,128]{1,0:T(8,128)(2,1)}) %reduce-scatter.9.cloned.1.call-update) | async-done | bytes 16400 | tf_op jit(solution)/shard_map/reduce_scatter | solution.py:79
  778.2 1.6 fusion.16
  780.0 71.7 %all-reduce.14.cloned.1.call-done = bf16[512,128]{0,1:T(8,128)(2,1)} async-done(((bf16[512,128]{0,1:T(8,128)(2,1)}), bf16[512,128]{0,1:T(8,128)(2,1)}) %all-reduce.14.cloned.1.call-update) | async-done | bytes 131088 | tf_op jit(solution)/shard_map/psum | solution.py:88
  851.7 1.2 pad_maximum_fusion
  852.9 1.4 gather_fusion.1
  854.3 1.5 fusion.7
  855.8 1.3 copy.43
  857.1 2.4 fusion.99
  862.3 19.0 %reduce-scatter.11.cloned.1.call-done = bf16[1,512,128]{2,1,0:T(8,128)(2,1)} async-done(((bf16[4,512,128]{2,1,0:T(8,128)(2,1)}), bf16[1,512,128]{2,1,0:T(8,128)(2,1)}) %reduce-scatter.11.cloned.1.call-update) | async-done | bytes 131088 | tf_op jit(solution)/shard_map/reduce_scatter | solution.py:99
  881.3 1.2 convolution_bitcast_fusion
  (151 shorter events, 22.7 us)
Async XLA Ops:
  7.2 12.3 %copy-start = (bf16[1,4,512,512]{3,2,1,0:T(8,128)(2,1)S(1)}, bf16[1,4,512,512]{3,2,1,0:T(8,128)(2,1)}, u32[]{:S(2)}) copy-start(bf16[1,4,512,512]{3,2,1,0:T(8,128)(2,1)} %param.12) | copy-start | bytes 6291460
  7.2 92.4 %all-reduce.18.cloned.1.call-start = ((), (), s32[]{:S(2)}) async-start(), calls=%async_computation.13 | async-start | bytes 1048576
  19.5 3.2 copy-start.15
  21.4 4.6 copy-start.17
  21.4 143.4 %copy-start.2 = (bf16[4,64,512]{2,1,0:T(8,128)(2,1)S(1)}, bf16[4,64,512]{2,1,0:T(8,128)(2,1)}, u32[]{:S(2)}) copy-start(bf16[4,64,512]{2,1,0:T(8,128)(2,1)} %param.16) | copy-start | bytes 786436
  22.7 111.4 %copy-start.14 = (bf16[4,64,128]{2,1,0:T(8,128)(2,1)S(1)}, bf16[4,64,128]{2,1,0:T(8,128)(2,1)}, u32[]{:S(2)}) copy-start(bf16[4,64,128]{2,1,0:T(8,128)(2,1)} %param.15) | copy-start | bytes 196612
  22.7 168.1 %copy-start.5 = (bf16[6,64,512]{2,1,0:T(8,128)(2,1)S(1)}, bf16[6,64,512]{2,1,0:T(8,128)(2,1)}, u32[]{:S(2)}) copy-start(bf16[6,64,512]{2,1,0:T(8,128)(2,1)} %param.17) | copy-start | bytes 1179652
  26.0 107.3 %all-reduce.16.cloned.1.call-start = ((), (), s32[]{:S(2)}) async-start(), calls=%async_computation.12 | async-start | bytes 131072 | tf_op jit(solution)/shard_map/psum | solution.py:43
  101.1 335.9 %all-reduce.8.cloned.1.call-start = ((), (), s32[]{:S(2)}) async-start(), calls=%async_computation.4 | async-start | bytes 262144 | tf_op jit(solution)/shard_map/psum | solution.py:88
  164.9 6.5 collective-permute-start
  171.4 6.4 collective-permute-start.1
  171.4 6.4 collective-permute-start.4
  177.9 6.4 collective-permute-start.2
  177.9 6.4 collective-permute-start.5
  184.3 6.4 collective-permute-start.3
  184.3 6.5 collective-permute-start.6
  222.1 6.5 collective-permute-start.7
  228.6 6.4 collective-permute-start.8
  228.6 6.4 collective-permute-start.11
  235.0 6.4 collective-permute-start.9
  235.0 6.9 collective-permute-start.12
  241.5 6.4 collective-permute-start.10
  241.9 6.2 collective-permute-start.13
  280.5 6.5 collective-permute-start.14
  287.0 6.4 collective-permute-start.15
  287.0 6.4 collective-permute-start.18
  293.4 6.4 collective-permute-start.16
  293.5 6.4 collective-permute-start.19
  299.9 6.4 collective-permute-start.17
  299.9 6.5 collective-permute-start.20
  307.8 406.4 %slice-start = ((bf16[6,64,512]{2,1,0:T(8,128)(2,1)}), bf16[2,64,512]{2,1,0:T(8,128)(2,1)S(1)}, s32[]{:S(2)}) async-start(bf16[6,64,512]{2,1,0:T(8,128)(2,1)} %param.17), calls=%async_computation.14 | async-start | bytes 262144 | tf_op jit(solution)/shard_map/slice | solution.py:72
  338.6 6.5 collective-permute-start.21
  345.1 17.7 %copy-start.10 = (bf16[64,128]{1,0:T(8,128)(2,1)}, bf16[64,128]{1,0:T(8,128)(2,1)S(1)}, u32[]{:S(2)}) copy-start(bf16[64,128]{1,0:T(8,128)(2,1)S(1)} %collective-permute-done.21) | copy-start | bytes 49156
  345.1 6.4 collective-permute-start.22
  345.1 6.4 collective-permute-start.25
  351.6 11.3 %copy-start.12 = (bf16[64,128]{1,0:T(8,128)(2,1)}, bf16[64,128]{1,0:T(8,128)(2,1)S(1)}, u32[]{:S(2)}) copy-start(bf16[64,128]{1,0:T(8,128)(2,1)S(1)} %collective-permute-done.22) | copy-start | bytes 49156
  351.6 6.4 collective-permute-start.23
  351.6 11.3 %copy-start.11 = (bf16[64,128]{1,0:T(8,128)(2,1)}, bf16[64,128]{1,0:T(8,128)(2,1)S(1)}, u32[]{:S(2)}) copy-start(bf16[64,128]{1,0:T(8,128)(2,1)S(1)} %collective-permute-done.25) | copy-start | bytes 49156
  351.6 6.4 collective-permute-start.26
  358.0 4.8 copy-start.13
  358.0 6.5 collective-permute-start.24
  358.0 10.9 %collective-permute-start.27 = (bf16[64,128]{1,0:T(8,128)(2,1)}, bf16[64,128]{1,0:T(8,128)(2,1)S(1)}, u32[]{:S(2)}, u32[]{:S(2)}) collective-permute-start(bf16[64,128]{1,0:T(8,128)(2,1)} %collective-permute-done.26), channel_id=1, source_target_pairs={{0,28},{4,0},{8,4},{12,8},{16,12},{20,16},{24,20},{28,24},{1,29},{... | collective-permute-start | bytes 49160 | tf_op jit(solution)/shard_map/ppermute | solution.py:16
  369.9 131.9 %reduce-scatter.5.cloned.1.call-start = ((), (), s32[]{:S(2)}) async-start(), calls=%async_computation.5 | async-start | bytes 147456 | tf_op jit(solution)/shard_map/reduce_scatter | solution.py:79
  437.9 413.9 %copy-start.3 = (bf16[64,128]{0,1:T(8,128)(2,1)}, bf16[64,128]{0,1:T(8,128)(2,1)S(1)}, u32[]{:S(2)}) copy-start(bf16[64,128]{0,1:T(8,128)(2,1)S(1)} %constant_dynamic-slice_fusion.2) | copy-start | bytes 49156
  438.8 136.3 %all-reduce.10.cloned.1.call-start = ((), (), s32[]{:S(2)}) async-start(), calls=%async_computation.6 | async-start | bytes 262144 | tf_op jit(solution)/shard_map/psum | solution.py:88
  503.4 136.4 %reduce-scatter.7.cloned.1.call-start = ((), (), s32[]{:S(2)}) async-start(), calls=%async_computation.7 | async-start | bytes 147456 | tf_op jit(solution)/shard_map/reduce_scatter | solution.py:79
  575.9 275.8 %copy-start.6 = (bf16[64,128]{0,1:T(8,128)(2,1)}, bf16[64,128]{0,1:T(8,128)(2,1)S(1)}, u32[]{:S(2)}) copy-start(bf16[64,128]{0,1:T(8,128)(2,1)S(1)} %constant_dynamic-slice_fusion.1) | copy-start | bytes 49156
  578.2 201.7 %copy-start.16 = (s32[1,4]{1,0:T(1,128)S(1)}, s32[1,4]{1,0:T(1,128)}, u32[]{:S(2)}) copy-start(s32[1,4]{1,0:T(1,128)} %param.13) | copy-start | bytes 52
  578.2 135.1 %all-reduce.12.cloned.1.call-start = ((), (), s32[]{:S(2)}) async-start(), calls=%async_computation.8 | async-start | bytes 262144 | tf_op jit(solution)/shard_map/psum | solution.py:88
  641.5 136.7 %reduce-scatter.9.cloned.1.call-start = ((), (), s32[]{:S(2)}) async-start(), calls=%async_computation.9 | async-start | bytes 147456 | tf_op jit(solution)/shard_map/reduce_scatter | solution.py:79
  714.2 137.6 %copy-start.8 = (bf16[64,128]{0,1:T(8,128)(2,1)}, bf16[64,128]{0,1:T(8,128)(2,1)S(1)}, u32[]{:S(2)}) copy-start(bf16[64,128]{0,1:T(8,128)(2,1)S(1)} %constant_dynamic-slice_fusion) | copy-start | bytes 49156
  715.9 135.8 %all-reduce.14.cloned.1.call-start = ((), (), s32[]{:S(2)}) async-start(), calls=%async_computation.10 | async-start | bytes 262144 | tf_op jit(solution)/shard_map/psum | solution.py:88
  779.9 101.4 %reduce-scatter.11.cloned.1.call-start = ((), (), s32[]{:S(2)}) async-start(), calls=%async_computation.11 | async-start | bytes 655360 | tf_op jit(solution)/shard_map/reduce_scatter | solution.py:99
  857.1 3.3 copy-start.4
  857.1 3.4 copy-start.7
  857.1 3.5 copy-start.9
  857.1 24.2 %copy-start.1 = (bf16[1,512,512]{2,1,0:T(8,128)(2,1)S(1)}, bf16[1,512,512]{2,1,0:T(8,128)(2,1)}, u32[]{:S(2)}) copy-start(bf16[1,512,512]{2,1,0:T(8,128)(2,1)} %param.11) | copy-start | bytes 1572868
Sparse Core Ops, SparseCore 0:
  26.1 73.4 all-reduce.17
  102.5 30.7 all-reduce.15
  370.0 66.9 all-reduce.7
  440.8 60.9 reduce-scatter.4
  505.5 69.5 all-reduce.9
  578.8 60.9 reduce-scatter.6
  643.8 69.5 all-reduce.11
  717.2 60.9 reduce-scatter.8
  782.2 69.5 all-reduce.13
  860.5 20.7 reduce-scatter.10
